TPU v7x, 512 devices: a whole 4x8x8 slice. The times are simulated.
512 devices in a mesh: grp: 16 (over x, z_lo), ep: 32 (over y, z_hi, core).
Axes of the slice: x: 4, y: 8, z: 8 (z_hi: 2, z_lo: 4; z = z_hi * 4 + z_lo), core: 2. Of those that a mesh axis runs over, the one named last changes fastest.
Arguments:
- slot_hidden: bfloat16 [65536, 8, 768], P(('grp', 'ep')), may hold values from -6 to 6
- expert_ids: int32 [65536, 8], P(('grp', 'ep')), may hold values from 0 to 63, all different within a row; in each aligned block of 128 rows (0 to 127, 128 to 255, ...) at most 24 rows name the same one
- gate_fixed: int32 [65536, 8], P(('grp', 'ep')), may hold values from 1 to 65535
- master: float32 [64, 768, 2048], P('ep', 'grp'), may hold values from -6 to 6
- moment_one: bfloat16 [64, 768, 2048], P('ep', 'grp'), may hold values from -3 to 3
- moment_two: bfloat16 [64, 768, 2048], P('ep', 'grp'), may hold values from 0.0099487305 to 2
- gradient: bfloat16 [64, 768, 2048], P('ep', 'grp'), may hold values from -6 to 6
Outputs:
- mixed: bfloat16 [65536, 2048], P(('grp', 'ep'))
- backup: float32 [64, 768, 2048], P('ep', 'grp')
Inputs may be any that keep to these rules, and one draw needn't show every extreme that they name: `expert_ids`: in each aligned block of 128 rows (the rows of one device) no expert is named by more than 24 rows, a bound that some block reaches; the 8 experts of a row differ.
All inputs are finite; a program needn't handle non-finite values.
Results may differ from a plain program's by a relative error of at most 0.0057.
Values may be sent and summed in bfloat16 or wider, within the bound.
No kernel may reach another device: no remote copies, remote signals or barrier semaphores. Data moves between devices by JAX's collectives and lax.ppermute only.
A program may use at most 64 MiB of HBM per device.

v0:
```python
import math
import jax
import jax.numpy as jnp
from jax import lax
from jax.sharding import Mesh
from jax.sharding import PartitionSpec as P

GRP = ("grp_0", "grp_1")
beta_one = 0.9
beta_two = 0.95
corr_one = 1.0 - 0.9**40
corr_two = 1.0 - 0.95**40
learn_rate = 0.05
decay_rate = 0.1
adam_eps = 1e-08
gate_unit = 65536.0


def adamw_step(master, moment_one, moment_two, gradient):
    widened = gradient.astype(jnp.float32)
    first_moment = beta_one * moment_one.astype(jnp.float32) + (1.0 - beta_one) * widened
    second_moment = beta_two * moment_two.astype(jnp.float32) + (1.0 - beta_two) * widened * widened
    return (
        first_moment / corr_one / (jnp.sqrt(second_moment / corr_two) + adam_eps)
        + decay_rate * master
    )


def slot_positions(ids, capacity):
    count = ids.shape[0]
    rows = lax.broadcasted_iota(jnp.int32, (count, count), 0)
    cols = lax.broadcasted_iota(jnp.int32, (count, count), 1)
    same = (ids[:, None] == ids[None, :]) & (cols < rows)
    slot_index = jnp.sum(same.astype(jnp.int32), axis=1)
    return ids * capacity + slot_index


def body(slot_hidden, expert_ids, gate_fixed, master, moment_one, moment_two, gradient):
    outer = lax.axis_size("grp_0")
    ranks = lax.axis_size("ep")
    local_experts = master.shape[0]
    experts = local_experts * ranks
    tok_count, top_count, hidden_width = slot_hidden.shape
    width = master.shape[2]
    capacity = max(2, tok_count * top_count // experts + tok_count * top_count // (2 * experts))
    slots = experts * capacity
    scaling = 1.0 / math.sqrt(hidden_width)
    step_dir = adamw_step(master, moment_one, moment_two, gradient)
    updated = master - learn_rate * step_dir
    weights = updated.astype(jnp.bfloat16)
    shift = outer // 2
    backup = lax.ppermute(step_dir, "grp_0", [(s, (s + shift) % outer) for s in range(outer)])
    pairs = tok_count * top_count
    positions = slot_positions(expert_ids.reshape(pairs), capacity)
    hidden_rows = slot_hidden.reshape(pairs, hidden_width)
    token_pos = positions.reshape(tok_count, top_count)
    high = (gate_fixed // 256).astype(jnp.float32) / 256.0
    low = (gate_fixed % 256).astype(jnp.float32) / gate_unit
    chunk = ranks * capacity
    column = lax.broadcasted_iota(jnp.int32, (chunk,), 0)
    slot_of = []
    arrived = []
    for local in range(local_experts):
        slot_of.append((column // capacity * local_experts + local) * capacity + column % capacity)
        placing = (positions[None, :] == slot_of[local][:, None]).astype(jnp.bfloat16)
        outgoing = jnp.dot(placing, hidden_rows, preferred_element_type=jnp.float32).astype(
            jnp.bfloat16
        )
        arrived.append(
            lax.all_to_all(
                outgoing.reshape(ranks, capacity, hidden_width),
                "ep",
                split_axis=0,
                concat_axis=0,
                tiled=True,
            )
        )
    gathered = []
    first_stage = []
    for local in range(local_experts):
        own = weights[local]
        if first_stage:
            own, _ = lax.optimization_barrier((own, arrived[0]))
        rows = lax.all_gather(own, "grp_1", axis=0, tiled=True)
        first_stage.append(rows)
        rows, tie = lax.optimization_barrier((rows, gathered[-1] if gathered else arrived[0]))
        if not gathered:
            arrived[0] = tie
        gathered.append(lax.all_gather(rows, "grp_0", axis=0, tiled=True))
    mixed = jnp.zeros((tok_count, width), jnp.float32)
    for local in range(local_experts):
        product = jnp.dot(
            arrived[local].reshape(chunk, hidden_width),
            gathered[local],
            preferred_element_type=jnp.float32,
        )
        results = (product * scaling).astype(jnp.bfloat16)
        if local + 1 < local_experts:
            results, _ = lax.optimization_barrier((results, first_stage[local + 1]))
        returned = lax.all_to_all(
            results.reshape(ranks, capacity, width), "ep", split_axis=0, concat_axis=0, tiled=True
        )
        returned = returned.reshape(chunk, width)
        hit = token_pos[:, :, None] == slot_of[local][None, None, :]
        weight = jnp.concatenate(
            [jnp.sum(jnp.where(hit, part[:, :, None], 0.0), axis=1) for part in (high, low)], axis=0
        )
        both = jnp.dot(weight.astype(jnp.bfloat16), returned, preferred_element_type=jnp.float32)
        mixed = mixed + both[:tok_count] + both[tok_count:]
    return (mixed.astype(jnp.bfloat16), backup)


def solution(mesh):
    torus = Mesh(mesh.devices.reshape(4, 4, mesh.shape["ep"]), ("grp_0", "grp_1", "ep"))
    tokens = P(GRP + ("ep",), None, None)
    pair_spec = P(GRP + ("ep",), None)
    state = P("ep", GRP, None)
    in_specs = (tokens, pair_spec, pair_spec, state, state, state, state)
    out_specs = (pair_spec, state)
    return jax.shard_map(body, mesh=torus, in_specs=in_specs, out_specs=out_specs, check_vma=False)
```

profile of v0, /device:TPU:188, one launch (start us, length us, event | category | flops | bytes accessed | tf_op | source)
XLA Modules:
  0.0 326.0 jit_solution(854978757086746772)
XLA Ops:
  7.2 0.9 copy.22
  8.1 0.1 eq.33
  8.2 0.5 convert_reduce_fusion
  8.7 2.5 fusion.15
  11.2 13.7 %all-to-all-start = ((bf16[32,24,768]{2,1,0:T(8,128)(2,1)}), bf16[32,24,768]{2,1,0:T(8,128)(2,1)S(1)}, u32[]{:S(2)}, u32[]{:S(2)}) async-start(bf16[32,24,768]{2,1,0:T(8,128)(2,1)} %bitcast.31), calls=%async_computation | async-start | bytes 2359296 | tf_op jit(solution)/shard_map/all_to_all | solution.py:70
  25.0 0.0 all-gather.4.cloned.1.call-start
  25.0 2.8 subtract_convert_fusion
  27.9 39.6 %all-gather = bf16[1,192,2048]{2,1,0:T(8,128)(2,1)} all-gather(bf16[1,48,2048]{2,1,0:T(8,128)(2,1)S(1)} %get-tuple-element.20), channel_id=2, replica_groups=mesh['grp_0'=4,'grp_1'=4,'ep'=32] {'grp_1'}, dimensions={1}, use_global_device_ids=true | all-gather | bytes 983040 | tf_op jit(solution)/shard_map/all_gather | solution.py:84
  67.4 0.0 all-gather.4.cloned.1.call-update
  67.5 2.5 fusion.20
  70.0 10.2 %all-to-all-start.2 = ((bf16[32,24,768]{2,1,0:T(8,128)(2,1)}), bf16[32,24,768]{2,1,0:T(8,128)(2,1)}, u32[]{:S(2)}, u32[]{:S(2)}) async-start(bf16[32,24,768]{2,1,0:T(8,128)(2,1)} %bitcast.30), calls=%async_computation.2 | async-start | bytes 2359296 | tf_op jit(solution)/shard_map/all_to_all | solution.py:70
  80.1 43.1 %all_gather.14 = bf16[192,2048]{1,0:T(8,128)(2,1)} all-gather(bf16[48,2048]{1,0:T(8,128)(2,1)S(1)} %get-tuple-element.9), channel_id=1, replica_groups=mesh['grp_0'=4,'grp_1'=4,'ep'=32] {'grp_1'}, dimensions={0}, use_global_device_ids=true | all-gather | bytes 983040 | tf_op jit(solution)/shard_map/all_gather | solution.py:84
  123.2 5.9 %multiply_convert_fusion.1 = bf16[768,2048]{1,0:T(8,128)(2,1)} fusion(bf16[768,768]{1,0:T(8,128)(2,1)S(1)} %bitcast.29, bf16[768,2048]{1,0:T(8,128)(2,1)} %all-gather.4.cloned.1.call-done), kind=kOutput, calls=%fused_computation.1 | convolution fusion | flops 2419064832 | bytes 7471104 | tf_op jit(solution)/shard_map/dot_general | solution.py:92
  129.2 9.0 %all-to-all-start.1 = ((bf16[32,24,2048]{2,1,0:T(8,128)(2,1)}), bf16[32,24,2048]{2,1,0:T(8,128)(2,1)}, u32[]{:S(2)}, u32[]{:S(2)}) async-start(bf16[32,24,2048]{2,1,0:T(8,128)(2,1)} %bitcast.27), calls=%async_computation.1 | async-start | bytes 6291456 | tf_op jit(solution)/shard_map/all_to_all | solution.py:100
  138.2 0.0 all-gather.6.cloned.1.call-start
  138.3 0.7 all-gather.6.cloned.1.call-update
  139.0 48.5 %all-gather.6.cloned.1.call-done = bf16[768,2048]{1,0:T(8,128)(2,1)} async-done(((bf16[192,2048]{1,0:T(8,128)(2,1)}), bf16[768,2048]{1,0:T(8,128)(2,1)}) %all-gather.6.cloned.1.call-update) | async-done | bytes 3145744 | tf_op jit(solution)/shard_map/all_gather | solution.py:89
  187.5 6.5 %multiply_convert_fusion = bf16[768,2048]{1,0:T(8,128)(2,1)} fusion(bf16[768,768]{1,0:T(8,128)(2,1)} %bitcast.8, bf16[768,2048]{1,0:T(8,128)(2,1)} %all-gather.6.cloned.1.call-done), kind=kOutput, calls=%fused_computation | convolution fusion | flops 2419064832 | bytes 7471104 | tf_op jit(solution)/shard_map/dot_general | solution.py:92
  194.0 27.2 %all-to-all-done.1 = bf16[32,24,2048]{2,1,0:T(8,128)(2,1)} async-done(((bf16[32,24,2048]{2,1,0:T(8,128)(2,1)}), bf16[32,24,2048]{2,1,0:T(8,128)(2,1)}, u32[]{:S(2)}, u32[]{:S(2)}) %all-to-all-start.1) | async-done | bytes 3145760 | tf_op jit(solution)/shard_map/all_to_all | solution.py:100
  221.3 9.3 %all-to-all-start.3 = ((bf16[32,24,2048]{2,1,0:T(8,128)(2,1)}), bf16[32,24,2048]{2,1,0:T(8,128)(2,1)}, u32[]{:S(2)}, u32[]{:S(2)}) async-start(bf16[32,24,2048]{2,1,0:T(8,128)(2,1)} %bitcast.26), calls=%async_computation.3 | async-start | bytes 6291456 | tf_op jit(solution)/shard_map/all_to_all | solution.py:100
  230.6 2.6 collective-permute-start
  233.2 0.1 reduce_sum.48
  233.4 0.8 copy.24
  234.1 0.7 copy.25
  234.8 0.7 copy.26
  235.6 4.6 %fusion.2 = (bf16[128,768]{1,0:T(8,128)(2,1)S(1)}, bf16[128,768]{1,0:T(8,128)(2,1)S(1)}, bf16[128,768]{1,0:T(8,128)(2,1)S(1)}, bf16[128,768]{1,0:T(8,128)(2,1)S(1)}) fusion(f32[128,8]{1,0:T(8,128)} %copy.26, s32[768]{0:T(1024)S(1)} %get-tuple-element.25, s32[128,8]{1,0:T(8,128)} %copy.24, s32[768]{0:T(1024)S(1)} %get-tuple-element.24, f32[128,8]{1,0:T(8,128)} %copy.25), kind=kLoop, calls=%fused_computation.10 | loop fusion | flops 7471104 | bytes 804864 | tf_op jit(solution)/shard_map/reduce_sum | solution.py:106
  240.2 13.4 %collective-permute-done = f32[2,48,2048]{2,1,0:T(8,128)S(1)} collective-permute-done((f32[2,48,2048]{2,1,0:T(8,128)S(1)}, f32[2,48,2048]{2,1,0:T(8,128)S(1)}, u32[]{:S(2)}, u32[]{:S(2)}) %collective-permute-start) | collective-permute-done | bytes 786464 | tf_op jit(solution)/shard_map/ppermute | solution.py:52
  253.6 4.2 %fusion.34 = f32[256,2048]{1,0:T(8,128)} fusion(bf16[768,2048]{1,0:T(8,128)(2,1)} %bitcast.6, bf16[128,768]{1,0:T(8,128)(2,1)S(1)} %get-tuple-element.14, bf16[128,768]{1,0:T(8,128)(2,1)S(1)} %get-tuple-element.17), kind=kOutput, calls=%fused_computation.40 | convolution fusion | flops 806092800 | bytes 5636096 | tf_op jit(solution)/shard_map/dot_general | solution.py:108
  257.8 56.4 %all-to-all-done.3 = bf16[32,24,2048]{2,1,0:T(8,128)(2,1)} async-done(((bf16[32,24,2048]{2,1,0:T(8,128)(2,1)}), bf16[32,24,2048]{2,1,0:T(8,128)(2,1)}, u32[]{:S(2)}, u32[]{:S(2)}) %all-to-all-start.3) | async-done | bytes 3145760 | tf_op jit(solution)/shard_map/all_to_all | solution.py:100
  314.2 3.0 fusion.38
  317.3 1.0 fusion.25
  318.3 0.9 copy.28
  (21 shorter events, 0.1 us)
Async XLA Ops:
  7.2 1.6 copy-start
  8.7 16.3 %copy-start.2 = (f32[2,48,2048]{2,1,0:T(8,128)S(1)}, f32[2,48,2048]{2,1,0:T(8,128)}, u32[]{:S(2)}) copy-start(f32[2,48,2048]{2,1,0:T(8,128)} %param.10) | copy-start | bytes 2359300
  11.2 56.2 %all-to-all-start = ((bf16[32,24,768]{2,1,0:T(8,128)(2,1)}), bf16[32,24,768]{2,1,0:T(8,128)(2,1)S(1)}, u32[]{:S(2)}, u32[]{:S(2)}) async-start(bf16[32,24,768]{2,1,0:T(8,128)(2,1)} %bitcast.31), calls=%async_computation | async-start | bytes 2359296 | tf_op jit(solution)/shard_map/all_to_all | solution.py:70
  25.0 98.3 %all-gather.4.cloned.1.call-start = ((), (), s32[]{:S(2)}) async-start(), calls=%async_computation.4 | async-start | bytes 3932160 | tf_op jit(solution)/shard_map/all_gather | solution.py:89
  70.0 59.2 %all-to-all-start.2 = ((bf16[32,24,768]{2,1,0:T(8,128)(2,1)}), bf16[32,24,768]{2,1,0:T(8,128)(2,1)}, u32[]{:S(2)}, u32[]{:S(2)}) async-start(bf16[32,24,768]{2,1,0:T(8,128)(2,1)} %bitcast.30), calls=%async_computation.2 | async-start | bytes 2359296 | tf_op jit(solution)/shard_map/all_to_all | solution.py:70
  129.2 92.1 %all-to-all-start.1 = ((bf16[32,24,2048]{2,1,0:T(8,128)(2,1)}), bf16[32,24,2048]{2,1,0:T(8,128)(2,1)}, u32[]{:S(2)}, u32[]{:S(2)}) async-start(bf16[32,24,2048]{2,1,0:T(8,128)(2,1)} %bitcast.27), calls=%async_computation.1 | async-start | bytes 6291456 | tf_op jit(solution)/shard_map/all_to_all | solution.py:100
  138.2 49.3 %all-gather.6.cloned.1.call-start = ((), (), s32[]{:S(2)}) async-start(), calls=%async_computation.5 | async-start | bytes 3932160 | tf_op jit(solution)/shard_map/all_gather | solution.py:89
  221.3 9.3 %copy-start.3 = (f32[2,48,2048]{2,1,0:T(8,128)S(1)}, f32[2,48,2048]{2,1,0:T(8,128)}, u32[]{:S(2)}) copy-start(f32[2,48,2048]{2,1,0:T(8,128)} %get-tuple-element.19) | copy-start | bytes 2359300
  221.3 12.1 %copy-start.4 = (s32[128,8]{0,1:T(8,128)S(1)}, s32[128,8]{0,1:T(8,128)}, u32[]{:S(2)}) copy-start(s32[128,8]{0,1:T(8,128)} %param.8) | copy-start | bytes 12292
  221.3 12.9 %copy-start.5 = (s32[128,8]{0,1:T(8,128)S(1)}, s32[128,8]{0,1:T(8,128)}, u32[]{:S(2)}) copy-start(s32[128,8]{0,1:T(8,128)} %param.9) | copy-start | bytes 12292
  221.3 93.0 %all-to-all-start.3 = ((bf16[32,24,2048]{2,1,0:T(8,128)(2,1)}), bf16[32,24,2048]{2,1,0:T(8,128)(2,1)}, u32[]{:S(2)}, u32[]{:S(2)}) async-start(bf16[32,24,2048]{2,1,0:T(8,128)(2,1)} %bitcast.26), calls=%async_computation.3 | async-start | bytes 6291456 | tf_op jit(solution)/shard_map/all_to_all | solution.py:100
  230.6 23.0 %collective-permute-start = (f32[2,48,2048]{2,1,0:T(8,128)S(1)}, f32[2,48,2048]{2,1,0:T(8,128)S(1)}, u32[]{:S(2)}, u32[]{:S(2)}) collective-permute-start(f32[2,48,2048]{2,1,0:T(8,128)S(1)} %copy-done.3), channel_id=1, source_target_pairs={{0,256},{128,384},{256,0},{384,128},{1,257},{129,385},{257,1},{385... | collective-permute-start | bytes 2359304 | tf_op jit(solution)/shard_map/ppermute | solution.py:52
  314.2 3.0 copy-start.1
Sparse Core Ops, SparseCore 0:
  67.6 44.2 all-gather.3
  141.1 46.2 all-gather.5
where the time goes:
time: 327 us; the launch traced here: 326 us
  waiting for transfers between devices  146 us (45%)
  blocking collectives  82.7 us (25%)
  starting transfers between devices  45 us (14%)
  matrix products  24.7 us (8%)
  between operations  14.2 us (4%)
  other arithmetic  9.01 us (3%)
  local copies, waits for them, and re-layouts  4.26 us (1%)
    all_to_all x2, waiting for transfers between devices, body(): lax.all_to_all(results.reshape(ranks, capacity, width), 'ep', split_axis=...  83.7 us
    all_gather x2, blocking collectives, body(): rows = lax.all_gather(own, 'grp_1', axis=0, tiled=True)  82.7 us
    all_gather x2, waiting for transfers between devices, body(): gathered.append(lax.all_gather(rows, 'grp_0', axis=0, tiled=True))  48.5 us
    all_to_all x2, starting transfers between devices, body(): lax.all_to_all(outgoing.reshape(ranks, capacity, hidden_width), 'ep', spl...  23.9 us
    all_to_all x2, starting transfers between devices, body(): lax.all_to_all(results.reshape(ranks, capacity, width), 'ep', split_axis=...  18.3 us
    ppermute x1, waiting for transfers between devices, body(): lax.ppermute(step_dir, 'grp_0', [(s, (s + shift) % outer) for s in range(...  13.4 us
    dot_general x2, matrix products, body(): jnp.dot(arrived[local].reshape(chunk, hidden_width), gathered[local], pre...  12.5 us
    dot_general x2, matrix products, body(): jnp.dot(weight.astype(jnp.bfloat16), returned, preferred_element_type=jnp...  7.24 us
  transfers between devices with their start and end apart: 7, of which 4 were waited for; matrix products, arithmetic and copies ran while one was open for 9% of the time, Pallas kernels for 0%

commit v1 on v0

--- a/solution.py
+++ b/solution.py
@@ -86,7 +86,18 @@
         rows, tie = lax.optimization_barrier((rows, gathered[-1] if gathered else arrived[0]))
         if not gathered:
             arrived[0] = tie
-        gathered.append(lax.all_gather(rows, "grp_0", axis=0, tiled=True))
+
+        def process_fields_on(raw):
+            part_next = lax.all_to_all(
+                jnp.stack([raw for _ in range(lax.psum(1, axis_name="grp_0"))], axis=0),
+                axis_name="grp_0",
+                split_axis=0,
+                concat_axis=0,
+            )
+            part_now = jnp.concatenate(part_next, 0)
+            return part_now
+
+        gathered.append(process_fields_on(rows))
     mixed = jnp.zeros((tok_count, width), jnp.float32)
     for local in range(local_experts):
         product = jnp.dot(

time: 327 us -> 392 us (1.20)
  the two profiles are of different devices: /device:TPU:188 before, /device:TPU:56 now
where the time goes in v1:
time: 392 us; the launch traced here: 391 us
  waiting for transfers between devices  209 us (53%)
  blocking collectives  83.3 us (21%)
  starting transfers between devices  55.5 us (14%)
  matrix products  24.6 us (6%)
  local copies, waits for them, and re-layouts  9.09 us (2%)
  other arithmetic  9.01 us (2%)
    all_to_all x2, waiting for transfers between devices, body(): lax.all_to_all(results.reshape(ranks, capacity, width), 'ep', split_axis=...  130 us
    all_gather x2, blocking collectives, body(): rows = lax.all_gather(own, 'grp_1', axis=0, tiled=True)  83.3 us
    all_to_all x2, waiting for transfers between devices, process_fields_on(): lax.all_to_all(jnp.stack([raw for _ in range(lax.psum(1, axis_name='grp_0...  65.4 us
    all_to_all x2, starting transfers between devices, body(): lax.all_to_all(outgoing.reshape(ranks, capacity, hidden_width), 'ep', spl...  24.6 us
    all_to_all x2, starting transfers between devices, body(): lax.all_to_all(results.reshape(ranks, capacity, width), 'ep', split_axis=...  18.9 us
    ppermute x1, waiting for transfers between devices, body(): lax.ppermute(step_dir, 'grp_0', [(s, (s + shift) % outer) for s in range(...  13.4 us
    dot_general x2, matrix products, body(): jnp.dot(arrived[local].reshape(chunk, hidden_width), gathered[local], pre...  12.4 us
    all_to_all x2, starting transfers between devices, process_fields_on(): lax.all_to_all(jnp.stack([raw for _ in range(lax.psum(1, axis_name='grp_0...  9.29 us
  transfers between devices with their start and end apart: 7, of which 5 were waited for; matrix products, arithmetic and copies ran while one was open for 8% of the time, Pallas kernels for 0%

profile of v1, /device:TPU:56, one launch (start us, length us, event | category | flops | bytes accessed | tf_op | source)
XLA Modules:
  0.0 391.5 jit_solution(1932060789856087801)
XLA Ops:
  0.7 0.9 copy.22
  1.7 0.5 convert_reduce_fusion
  2.2 2.5 fusion.15
  4.7 15.5 %all-to-all-start = ((bf16[32,24,768]{2,1,0:T(8,128)(2,1)}), bf16[32,24,768]{2,1,0:T(8,128)(2,1)S(1)}, u32[]{:S(2)}, u32[]{:S(2)}) async-start(bf16[32,24,768]{2,1,0:T(8,128)(2,1)} %bitcast.32), calls=%async_computation | async-start | bytes 2359296 | tf_op jit(solution)/shard_map/all_to_all | solution.py:70
  20.3 2.8 subtract_convert_fusion
  23.1 0.7 fusion.60
  23.8 40.5 %all-gather = bf16[1,192,2048]{2,1,0:T(8,128)(2,1)S(1)} all-gather(bf16[1,48,2048]{2,1,0:T(8,128)(2,1)S(1)} %get-tuple-element.20), channel_id=2, replica_groups=mesh['grp_0'=4,'grp_1'=4,'ep'=32] {'grp_1'}, dimensions={1}, use_global_device_ids=true | all-gather | bytes 983040 | tf_op jit(solution)/shard_map/all_gather | solution.py:84
  64.2 2.1 stack.4
  66.3 4.6 %all-to-all-start.1 = ((bf16[4,192,2048]{2,1,0:T(8,128)(2,1)}), bf16[4,192,2048]{2,1,0:T(8,128)(2,1)}, u32[]{:S(2)}, u32[]{:S(2)}) async-start(bf16[4,192,2048]{2,1,0:T(8,128)(2,1)} %stack.4), calls=%async_computation.1 | async-start | bytes 6291456 | tf_op jit(solution)/shard_map/all_to_all | solution.py:91
  71.0 2.5 fusion.20
  73.4 34.9 %all-to-all-done.1 = bf16[4,192,2048]{2,1,0:T(8,128)(2,1)} async-done(((bf16[4,192,2048]{2,1,0:T(8,128)(2,1)}), bf16[4,192,2048]{2,1,0:T(8,128)(2,1)}, u32[]{:S(2)}, u32[]{:S(2)}) %all-to-all-start.1) | async-done | bytes 3145760 | tf_op jit(solution)/shard_map/all_to_all | solution.py:91
  108.3 9.1 %all-to-all-start.3 = ((bf16[32,24,768]{2,1,0:T(8,128)(2,1)}), bf16[32,24,768]{2,1,0:T(8,128)(2,1)}, u32[]{:S(2)}, u32[]{:S(2)}) async-start(bf16[32,24,768]{2,1,0:T(8,128)(2,1)} %bitcast.33), calls=%async_computation.3 | async-start | bytes 2359296 | tf_op jit(solution)/shard_map/all_to_all | solution.py:70
  117.4 42.8 %all_gather.7 = bf16[192,2048]{1,0:T(8,128)(2,1)S(1)} all-gather(bf16[48,2048]{1,0:T(8,128)(2,1)} %get-tuple-element.9), channel_id=1, replica_groups=mesh['grp_0'=4,'grp_1'=4,'ep'=32] {'grp_1'}, dimensions={0}, use_global_device_ids=true | all-gather | bytes 983040 | tf_op jit(solution)/shard_map/all_gather | solution.py:84
  160.2 2.1 stack.5
  162.3 4.7 %all-to-all-start.4 = ((bf16[4,192,2048]{2,1,0:T(8,128)(2,1)}), bf16[4,192,2048]{2,1,0:T(8,128)(2,1)}, u32[]{:S(2)}, u32[]{:S(2)}) async-start(bf16[4,192,2048]{2,1,0:T(8,128)(2,1)} %stack.5), calls=%async_computation.4 | async-start | bytes 6291456 | tf_op jit(solution)/shard_map/all_to_all | solution.py:91
  166.9 5.9 %multiply_convert_fusion.1 = bf16[768,2048]{1,0:T(8,128)(2,1)} fusion(bf16[768,768]{1,0:T(8,128)(2,1)S(1)} %bitcast.31, bf16[768,2048]{1,0:T(8,128)(2,1)} %bitcast.4), kind=kOutput, calls=%fused_computation.1 | convolution fusion | flops 2419064832 | bytes 7471104 | tf_op jit(solution)/shard_map/dot_general | solution.py:103
  172.8 30.5 %all-to-all-done.4 = bf16[4,192,2048]{2,1,0:T(8,128)(2,1)} async-done(((bf16[4,192,2048]{2,1,0:T(8,128)(2,1)}), bf16[4,192,2048]{2,1,0:T(8,128)(2,1)}, u32[]{:S(2)}, u32[]{:S(2)}) %all-to-all-start.4) | async-done | bytes 3145760 | tf_op jit(solution)/shard_map/all_to_all | solution.py:91
  203.3 9.6 %all-to-all-start.2 = ((bf16[32,24,2048]{2,1,0:T(8,128)(2,1)}), bf16[32,24,2048]{2,1,0:T(8,128)(2,1)}, u32[]{:S(2)}, u32[]{:S(2)}) async-start(bf16[32,24,2048]{2,1,0:T(8,128)(2,1)} %bitcast.29), calls=%async_computation.2 | async-start | bytes 6291456 | tf_op jit(solution)/shard_map/all_to_all | solution.py:111
  212.9 6.5 %multiply_convert_fusion = bf16[768,2048]{1,0:T(8,128)(2,1)} fusion(bf16[768,768]{1,0:T(8,128)(2,1)} %bitcast.9, bf16[768,2048]{1,0:T(8,128)(2,1)} %bitcast.10), kind=kOutput, calls=%fused_computation | convolution fusion | flops 2419064832 | bytes 7471104 | tf_op jit(solution)/shard_map/dot_general | solution.py:103
  219.5 74.3 %all-to-all-done.2 = bf16[32,24,2048]{2,1,0:T(8,128)(2,1)} async-done(((bf16[32,24,2048]{2,1,0:T(8,128)(2,1)}), bf16[32,24,2048]{2,1,0:T(8,128)(2,1)}, u32[]{:S(2)}, u32[]{:S(2)}) %all-to-all-start.2) | async-done | bytes 3145760 | tf_op jit(solution)/shard_map/all_to_all | solution.py:111
  293.8 9.3 %all-to-all-start.5 = ((bf16[32,24,2048]{2,1,0:T(8,128)(2,1)}), bf16[32,24,2048]{2,1,0:T(8,128)(2,1)}, u32[]{:S(2)}, u32[]{:S(2)}) async-start(bf16[32,24,2048]{2,1,0:T(8,128)(2,1)} %bitcast.28), calls=%async_computation.5 | async-start | bytes 6291456 | tf_op jit(solution)/shard_map/all_to_all | solution.py:111
  303.1 2.6 collective-permute-start
  305.9 0.7 copy.25
  306.6 0.7 copy.26
  307.4 0.8 copy.24
  308.2 4.6 %fusion.2 = (bf16[128,768]{1,0:T(8,128)(2,1)S(1)}, bf16[128,768]{1,0:T(8,128)(2,1)S(1)}, bf16[128,768]{1,0:T(8,128)(2,1)S(1)}, bf16[128,768]{1,0:T(8,128)(2,1)S(1)}) fusion(f32[128,8]{1,0:T(8,128)} %copy.26, s32[768]{0:T(1024)S(1)} %get-tuple-element.25, s32[128,8]{1,0:T(8,128)} %copy.24, s32[768]{0:T(1024)S(1)} %get-tuple-element.24, f32[128,8]{1,0:T(8,128)} %copy.25), kind=kLoop, calls=%fused_computation.10 | loop fusion | flops 7471104 | bytes 804864 | tf_op jit(solution)/shard_map/reduce_sum | solution.py:117
  312.8 13.4 %collective-permute-done = f32[2,48,2048]{2,1,0:T(8,128)S(1)} collective-permute-done((f32[2,48,2048]{2,1,0:T(8,128)S(1)}, f32[2,48,2048]{2,1,0:T(8,128)S(1)}, u32[]{:S(2)}, u32[]{:S(2)}) %collective-permute-start) | collective-permute-done | bytes 786464 | tf_op jit(solution)/shard_map/ppermute | solution.py:52
  326.1 4.2 %fusion.34 = f32[256,2048]{1,0:T(8,128)} fusion(bf16[768,2048]{1,0:T(8,128)(2,1)} %bitcast.7, bf16[128,768]{1,0:T(8,128)(2,1)S(1)} %get-tuple-element.14, bf16[128,768]{1,0:T(8,128)(2,1)S(1)} %get-tuple-element.17), kind=kOutput, calls=%fused_computation.40 | convolution fusion | flops 806092800 | bytes 5636096 | tf_op jit(solution)/shard_map/dot_general | solution.py:119
  330.4 56.2 %all-to-all-done.5 = bf16[32,24,2048]{2,1,0:T(8,128)(2,1)} async-done(((bf16[32,24,2048]{2,1,0:T(8,128)(2,1)}), bf16[32,24,2048]{2,1,0:T(8,128)(2,1)}, u32[]{:S(2)}, u32[]{:S(2)}) %all-to-all-start.5) | async-done | bytes 3145760 | tf_op jit(solution)/shard_map/all_to_all | solution.py:111
  386.5 3.0 fusion.38
  389.6 1.0 fusion.25
  390.6 0.9 copy.28
  (21 shorter events, 0.3 us)
Async XLA Ops:
  0.6 1.6 copy-start
  2.2 18.0 %copy-start.2 = (f32[2,48,2048]{2,1,0:T(8,128)S(1)}, f32[2,48,2048]{2,1,0:T(8,128)}, u32[]{:S(2)}) copy-start(f32[2,48,2048]{2,1,0:T(8,128)} %param.10) | copy-start | bytes 2359300
  4.7 59.5 %all-to-all-start = ((bf16[32,24,768]{2,1,0:T(8,128)(2,1)}), bf16[32,24,768]{2,1,0:T(8,128)(2,1)S(1)}, u32[]{:S(2)}, u32[]{:S(2)}) async-start(bf16[32,24,768]{2,1,0:T(8,128)(2,1)} %bitcast.32), calls=%async_computation | async-start | bytes 2359296 | tf_op jit(solution)/shard_map/all_to_all | solution.py:70
  66.3 42.0 %all-to-all-start.1 = ((bf16[4,192,2048]{2,1,0:T(8,128)(2,1)}), bf16[4,192,2048]{2,1,0:T(8,128)(2,1)}, u32[]{:S(2)}, u32[]{:S(2)}) async-start(bf16[4,192,2048]{2,1,0:T(8,128)(2,1)} %stack.4), calls=%async_computation.1 | async-start | bytes 6291456 | tf_op jit(solution)/shard_map/all_to_all | solution.py:91
  108.3 51.9 %all-to-all-start.3 = ((bf16[32,24,768]{2,1,0:T(8,128)(2,1)}), bf16[32,24,768]{2,1,0:T(8,128)(2,1)}, u32[]{:S(2)}, u32[]{:S(2)}) async-start(bf16[32,24,768]{2,1,0:T(8,128)(2,1)} %bitcast.33), calls=%async_computation.3 | async-start | bytes 2359296 | tf_op jit(solution)/shard_map/all_to_all | solution.py:70
  162.3 41.0 %all-to-all-start.4 = ((bf16[4,192,2048]{2,1,0:T(8,128)(2,1)}), bf16[4,192,2048]{2,1,0:T(8,128)(2,1)}, u32[]{:S(2)}, u32[]{:S(2)}) async-start(bf16[4,192,2048]{2,1,0:T(8,128)(2,1)} %stack.5), calls=%async_computation.4 | async-start | bytes 6291456 | tf_op jit(solution)/shard_map/all_to_all | solution.py:91
  203.3 90.5 %all-to-all-start.2 = ((bf16[32,24,2048]{2,1,0:T(8,128)(2,1)}), bf16[32,24,2048]{2,1,0:T(8,128)(2,1)}, u32[]{:S(2)}, u32[]{:S(2)}) async-start(bf16[32,24,2048]{2,1,0:T(8,128)(2,1)} %bitcast.29), calls=%async_computation.2 | async-start | bytes 6291456 | tf_op jit(solution)/shard_map/all_to_all | solution.py:111
  293.8 9.3 %copy-start.3 = (f32[2,48,2048]{2,1,0:T(8,128)S(1)}, f32[2,48,2048]{2,1,0:T(8,128)}, u32[]{:S(2)}) copy-start(f32[2,48,2048]{2,1,0:T(8,128)} %get-tuple-element.19) | copy-start | bytes 2359300
  293.8 12.1 %copy-start.5 = (s32[128,8]{0,1:T(8,128)S(1)}, s32[128,8]{0,1:T(8,128)}, u32[]{:S(2)}) copy-start(s32[128,8]{0,1:T(8,128)} %param.9) | copy-start | bytes 12292
  293.8 13.6 %copy-start.4 = (s32[128,8]{0,1:T(8,128)S(1)}, s32[128,8]{0,1:T(8,128)}, u32[]{:S(2)}) copy-start(s32[128,8]{0,1:T(8,128)} %param.8) | copy-start | bytes 12292
  293.8 92.7 %all-to-all-start.5 = ((bf16[32,24,2048]{2,1,0:T(8,128)(2,1)}), bf16[32,24,2048]{2,1,0:T(8,128)(2,1)}, u32[]{:S(2)}, u32[]{:S(2)}) async-start(bf16[32,24,2048]{2,1,0:T(8,128)(2,1)} %bitcast.28), calls=%async_computation.5 | async-start | bytes 6291456 | tf_op jit(solution)/shard_map/all_to_all | solution.py:111
  303.1 23.0 %collective-permute-start = (f32[2,48,2048]{2,1,0:T(8,128)S(1)}, f32[2,48,2048]{2,1,0:T(8,128)S(1)}, u32[]{:S(2)}, u32[]{:S(2)}) collective-permute-start(f32[2,48,2048]{2,1,0:T(8,128)S(1)} %copy-done.3), channel_id=1, source_target_pairs={{0,256},{128,384},{256,0},{384,128},{1,257},{129,385},{257,1},{385... | collective-permute-start | bytes 2359304 | tf_op jit(solution)/shard_map/ppermute | solution.py:52
  386.5 3.0 copy-start.1
